TPU v7x, 32 devices: a whole 2x2x4 slice. The times are simulated.
32 devices in a mesh: seq: 4 (over y, x), batch: 8 (over z, core).
Axes of the slice: x: 2, y: 2, z: 4, core: 2. Of those that a mesh axis runs over, the one named last changes fastest.
Arguments:
- feats: bfloat16 [768, 4096], P('seq', 'batch'), parts along dimension 1, may hold values from -6 to 6
- qkv_weight: bfloat16 [768, 2304], replicated, may hold values from -0.21875 to 0.21875
- beta_weight: bfloat16 [768, 6], replicated, may hold values from -0.21875 to 0.21875
- beta_bias: float32 [6], replicated, may hold values from -7 to 0.5
- out_gain: float32 [768], replicated, may hold values from 0.1 to 1.9
Outputs:
- mixed: bfloat16 [4096, 768], P(('batch', 'seq')), parts along dimension 0
There are 8 independent parts, one for each index of `batch`. A program takes and returns all parts, laid end to end along the dimension named above; an argument that names none is the same for every part. Nothing has to cross between parts.
All inputs are finite; a program needn't handle non-finite values.
Results may differ from a plain program's by a relative error of at most 0.012.
Values may be sent and summed in bfloat16 or wider, within the bound.
No kernel may reach another device: no remote copies, remote signals or barrier semaphores. Data moves between devices by JAX's collectives and lax.ppermute only.
A program may use at most 64 MiB of HBM per device.

v0:
```python
import jax
import jax.numpy as jnp
from jax import lax
from jax.sharding import PartitionSpec as P

HEADS = 6
HD = 128
GROUP = 64
HIGHEST_ACCURACY = lax.Precision.HIGHEST


def entering(value, axis, join, neutral):
    count, mine = (lax.axis_size(axis), lax.axis_index(axis))
    pieces = jax.tree.map(lambda part: lax.all_gather(part, axis), value)
    running = jax.tree.map(
        lambda part, zero: jnp.full_like(part, 0) + jnp.asarray(zero, part.dtype), value, neutral
    )

    def turn(position, running):
        longer = join(running, jax.tree.map(lambda part: part[position], pieces))
        return jax.tree.map(lambda new, old: jnp.where(position < mine, new, old), longer, running)

    return lax.fori_loop(0, count - 1, turn, running)


def unit_inverse(gram):
    eye_block = jnp.eye(gram.shape[-1], dtype=jnp.float32)
    negated = -jnp.tril(gram, -1)
    inverse = eye_block + negated
    power = negated
    for level in range(5):
        power = jnp.einsum("nhij,nhjk->nhik", power, power, precision=HIGHEST_ACCURACY)
        inverse = inverse + jnp.einsum(
            "nhij,nhjk->nhik", inverse, power, precision=HIGHEST_ACCURACY
        )
    return inverse


def prepare(qkv, beta):
    rows = qkv.shape[0]
    blocks_count = rows // GROUP
    pieces = qkv.astype(jnp.float32).reshape(rows, 3, HEADS, HD)
    query = pieces[:, 0]
    keys = pieces[:, 1]
    values = pieces[:, 2]
    query = query * lax.rsqrt(jnp.sum(query * query, -1, keepdims=True) + 1e-06)
    keys = keys * lax.rsqrt(jnp.sum(keys * keys, -1, keepdims=True) + 1e-06)

    def blocks(arr):
        return arr.reshape(blocks_count, GROUP, HEADS, arr.shape[-1]).transpose(0, 2, 1, 3)

    query = blocks(query)
    keys = blocks(keys)
    values = blocks(values)
    rates = blocks(beta[:, :, None])
    weighted = keys * rates
    gram = jnp.einsum("nhik,nhjk->nhij", weighted, keys, precision=HIGHEST_ACCURACY)
    inverse = unit_inverse(gram)
    right = jnp.concatenate([weighted, values * rates], -1)
    solved = jnp.einsum("nhij,nhjk->nhik", inverse, right, precision=HIGHEST_ACCURACY)
    wfac = solved[..., :HD]
    ufac = solved[..., HD:]
    scores = jnp.tril(jnp.einsum("nhik,nhjk->nhij", query, keys, precision=HIGHEST_ACCURACY))
    return (query, keys, wfac, ufac, scores)


def finish(outputs, out_gain):
    rows = outputs.shape[0] * GROUP
    flat = outputs.transpose(0, 2, 1, 3).reshape(rows, HEADS, HD)
    power = jnp.mean(flat * flat, -1, keepdims=True) + 1e-06
    normed = flat * lax.rsqrt(power) * out_gain.reshape(HEADS, HD)
    return normed.reshape(rows, HEADS * HD).astype(jnp.bfloat16)


def compose(early, late):
    first_move, first_offset = early
    second_move, second_offset = late
    move = jnp.einsum("hij,hjk->hik", second_move, first_move, precision=HIGHEST_ACCURACY)
    offset = (
        jnp.einsum("hij,hjk->hik", second_move, first_offset, precision=HIGHEST_ACCURACY)
        + second_offset
    )
    return (move, offset)


def body(feats, qkv_weight, beta_weight, beta_bias, out_gain):
    local = lax.all_to_all(feats, "seq", split_axis=1, concat_axis=0, tiled=True)
    qkv = lax.dot_general(
        local, qkv_weight, (((0,), (0,)), ((), ())), preferred_element_type=jnp.float32
    ).astype(jnp.bfloat16)
    logits = lax.dot_general(
        local, beta_weight, (((0,), (0,)), ((), ())), preferred_element_type=jnp.float32
    )
    beta = jax.nn.sigmoid(logits + beta_bias)
    query, keys, wfac, ufac, scores = prepare(qkv, beta)
    eye_heads = jnp.broadcast_to(jnp.eye(HD, dtype=jnp.float32), (HEADS, HD, HD))
    empty = jnp.zeros((HEADS, HD, HD), jnp.float32)

    def first_pass(joint_matrix, item):
        query_block, key_block, weight_block, update_block, state_block = item
        held_value = jnp.einsum(
            "rnf,rfw->rnw", weight_block, joint_matrix, precision=HIGHEST_ACCURACY
        )
        carried_state = joint_matrix[..., HD:]
        residual_value = update_block - held_value[..., HD:]
        output_rows = jnp.einsum(
            "rnf,rfw->rnw", query_block, carried_state, precision=HIGHEST_ACCURACY
        ) + jnp.einsum("fco,fop->fcp", state_block, residual_value, precision=HIGHEST_ACCURACY)
        target_value = jnp.concatenate([-held_value[..., :HD], residual_value], -1)
        joint_matrix = joint_matrix + jnp.einsum(
            "mjr,mjz->mrz", key_block, target_value, precision=HIGHEST_ACCURACY
        )
        return (joint_matrix, output_rows)

    joint_start = jnp.concatenate([eye_heads, empty], -1)
    joint_matrix, local_out = lax.scan(first_pass, joint_start, (query, keys, wfac, ufac, scores))
    moves = joint_matrix[..., :HD]
    offsets = joint_matrix[..., HD:]
    prior = entering((moves, offsets), "seq", compose, (eye_heads, empty))
    incoming = prior[1]

    def second_pass(loop_carry, item):
        query_block, key_block, weight_block, state_block = item
        held_value = jnp.einsum(
            "rnf,rfw->rnw", weight_block, loop_carry, precision=HIGHEST_ACCURACY
        )
        output_rows = jnp.einsum(
            "rnf,rfw->rnw", query_block, loop_carry, precision=HIGHEST_ACCURACY
        ) - jnp.einsum("fco,fop->fcp", state_block, held_value, precision=HIGHEST_ACCURACY)
        loop_carry = loop_carry - jnp.einsum(
            "mjr,mjz->mrz", key_block, held_value, precision=HIGHEST_ACCURACY
        )
        return (loop_carry, output_rows)

    final_carry, added_out = lax.scan(second_pass, incoming, (query, keys, wfac, scores))
    return finish(local_out + added_out, out_gain)


def solution(mesh):
    placed = (P("seq", "batch"), P(), P(), P(), P())
    return jax.shard_map(
        body, mesh=mesh, in_specs=placed, out_specs=P(("batch", "seq"), None), check_vma=False
    )
```

profile of v0, /device:TPU:0, one launch (start us, length us, event | category | flops | bytes accessed | tf_op | source)
XLA Modules:
  0.0 174.5 jit_solution(12034097138395976783)
XLA Ops:
  6.5 1.8 %copy_bitcast_fusion = bf16[192,4,128]{2,0,1:T(8,128)(2,1)} fusion(bf16[192,512]{1,0:T(8,128)(2,1)} %param.11), kind=kLoop, calls=%fused_computation.83 | loop fusion | bytes 393216 | tf_op jit(solution)/shard_map/all_to_all | solution.py:87
  8.3 5.2 %all-to-all-start = ((bf16[192,4,128]{2,0,1:T(8,128)(2,1)}), bf16[192,4,128]{2,0,1:T(8,128)(2,1)}, u32[]{:S(2)}, u32[]{:S(2)}) async-start(bf16[192,4,128]{2,0,1:T(8,128)(2,1)} %copy_bitcast_fusion), calls=%async_computation | async-start | bytes 393216 | tf_op jit(solution)/shard_map/all_to_all | solution.py:87
  17.3 1.5 all-to-all-done
  18.8 2.6 %fusion.45 = f32[128,2304]{1,0:T(8,128)} fusion(bf16[768,128]{1,0:T(8,128)(2,1)} %bitcast.12, bf16[768,2304]{1,0:T(8,128)(2,1)S(1)} %copy-done), kind=kOutput, calls=%fused_computation.53 | convolution fusion | flops 453574656 | bytes 4915200 | tf_op jit(solution)/shard_map/dot_general | solution.py:88
  21.4 2.7 %copy.50 = f32[128,2304]{0,1:T(8,128)} copy(f32[128,2304]{1,0:T(8,128)} %fusion.45) | data formatting | bytes 2359296 | tf_op jit(solution)/shard_map/reshape | solution.py:42
  24.1 2.3 %multiply_reduce_fusion.1 = (f32[128,6]{0,1:T(8,128)S(1)}, f32[128,6]{0,1:T(8,128)S(1)}, f32[128,1,6,128]{0,3,2,1:T(8,128)}, f32[128,1,6,128]{0,3,2,1:T(8,128)}, f32[128,1,6,128]{0,3,2,1:T(8,128)}) fusion(f32[128,3,6,128]{0,3,2,1:T(8,128)} %bitcast.151), kind=kLoop, calls=%fused_computation.80 | loop fusion | flops 391680 | bytes 2365440 | tf_op jit(solution)/shard_map/reduce_sum | solution.py:46
  28.3 1.9 %copy.51 = f32[128,1,6,128]{3,0,2,1:T(8,128)} copy(f32[128,1,6,128]{0,3,2,1:T(8,128)} %get-tuple-element.311) | data formatting | bytes 786432 | tf_op jit(solution)/shard_map/slice | solution.py:44
  30.2 1.9 %copy.55 = f32[128,1,6,128]{3,0,2,1:T(8,128)} copy(f32[128,1,6,128]{0,3,2,1:T(8,128)} %get-tuple-element.310) | data formatting | bytes 786432 | tf_op jit(solution)/shard_map/slice | solution.py:45
  32.2 1.7 fusion.50
  46.0 1.9 %copy.57 = f32[128,1,6,128]{3,0,2,1:T(8,128)} copy(f32[128,1,6,128]{0,3,2,1:T(8,128)} %get-tuple-element.309) | data formatting | bytes 786432 | tf_op jit(solution)/shard_map/slice | solution.py:43
  52.3 16.6 %while.38 = (s32[]{:T(128)}, f32[6,128,256]{2,1,0:T(8,128)}, f32[2,6,64,128]{3,2,1,0:T(8,128)}, f32[2,6,64,128]{3,2,1,0:T(8,128)}, f32[2,6,64,128]{3,2,1,0:T(8,1...) while((s32[]{:T(128)}, f32[6,128,256]{2,1,0:T(8,128)}, ...), condition=%wide.region_3.4_spmd, body=%wide.region_2.3_spmd.sunk | while | flops 415678464 | bytes 10029241 | solution.py:116
  52.3 1.9 %fusion.138 = f32[6,64,256]{2,1,0:T(8,128)S(1)} fusion(f32[6,128,256]{2,1,0:T(8,128)} %get-tuple-element.456, f32[2,6,64,128]{3,2,1,0:T(8,128)} %get-tuple-element.468, s32[]{:T(128)} %get-tuple-element.455), kind=kOutput, calls=%fused_computation.13.clone.1 | convolution fusion | flops 150994944 | bytes 1376768 | tf_op jit(solution)/shard_map/while/body/eval_jaxpr/rnf,rfw->rnw/dot_general | solution.py:101
  56.7 2.9 %convolution_add_fusion.10 = f32[6,128,256]{2,1,0:T(8,128)} fusion(f32[6,128,256]{2,1,0:T(8,128)} %get-tuple-element.456, f32[6,64,128]{2,1,0:T(8,128)S(1)} %get-tuple-element.432, f32[6,64,128]{2,1,0:T(8,128)S(1)} %get-tuple-element.433, f32[2,6,64,128]{3,2,1,0:T(8,128)S(1)} %copy-done.3, s32[]{:T(128)} %get-tuple-element.455), kind=kOutput, calls=%fused_computation.clone.1 | convolution fusion | flops 151289856 | bytes 2162692 | tf_op jit(solution)/shard_map/while/body/eval_jaxpr/mjr,mjz->mrz/dot_general | solution.py:110
  60.6 1.9 %fusion.138 = f32[6,64,256]{2,1,0:T(8,128)S(1)} fusion(f32[6,128,256]{2,1,0:T(8,128)} %get-tuple-element.456, f32[2,6,64,128]{3,2,1,0:T(8,128)} %get-tuple-element.468, s32[]{:T(128)} %get-tuple-element.455), kind=kOutput, calls=%fused_computation.13.clone.1 | convolution fusion | flops 150994944 | bytes 1376768 | tf_op jit(solution)/shard_map/while/body/eval_jaxpr/rnf,rfw->rnw/dot_general | solution.py:101
  65.0 2.9 %convolution_add_fusion.10 = f32[6,128,256]{2,1,0:T(8,128)} fusion(f32[6,128,256]{2,1,0:T(8,128)} %get-tuple-element.456, f32[6,64,128]{2,1,0:T(8,128)S(1)} %get-tuple-element.432, f32[6,64,128]{2,1,0:T(8,128)S(1)} %get-tuple-element.433, f32[2,6,64,128]{3,2,1,0:T(8,128)S(1)} %copy-done.3, s32[]{:T(128)} %get-tuple-element.455), kind=kOutput, calls=%fused_computation.clone.1 | convolution fusion | flops 151289856 | bytes 2162692 | tf_op jit(solution)/shard_map/while/body/eval_jaxpr/mjr,mjz->mrz/dot_general | solution.py:110
  68.9 2.1 %fusion.65 = (f32[6,128,128]{2,1,0:T(8,128)}, f32[6,128,128]{2,1,0:T(8,128)}) fusion(f32[6,128,256]{2,1,0:T(8,128)} %get-tuple-element.180), kind=kLoop, calls=%fused_computation.98 | loop fusion | bytes 1572864 | tf_op jit(solution)/shard_map/slice | solution.py:118
  71.8 30.7 %all-gather.5.cloned.1.call-done = f32[24,128,128]{2,1,0:T(8,128)} async-done(((f32[6,128,128]{2,1,0:T(8,128)}), f32[24,128,128]{2,1,0:T(8,128)}) %all-gather.5.cloned.1.call-update) | async-done | bytes 1572880 | tf_op jit(solution)/shard_map/all_gather | solution.py:14
  102.4 32.7 %all-gather.7.cloned.1.call-done = f32[24,128,128]{2,1,0:T(8,128)} async-done(((f32[6,128,128]{2,1,0:T(8,128)}), f32[24,128,128]{2,1,0:T(8,128)}) %all-gather.7.cloned.1.call-update) | async-done | bytes 1572880 | tf_op jit(solution)/shard_map/all_gather | solution.py:14
  135.1 10.2 %while.40 = (s32[]{:T(128)}, f32[6,128,128]{2,1,0:T(8,128)}, s32[]{:T(128)}, f32[4,6,128,128]{3,2,1,0:T(8,128)}, f32[4,6,128,128]{3,2,1,0:T(8,128)}, /*index=5*/s32[]{:T(128)}, s32[]{:T(128)}) while((s32[]{:T(128)}, f32[6,128,128]{2,1,0:T(8,128)}, s32[]{:T(128)}, f32[4,6,128,128]{3,2,1,0:T(8,128)}, f32[4,6,128,128]{3,2,1,0:T(8,128)}, ...), condition=%wide.region_5.6_spmd.clone, body=%wide.region_4.5_spmd.clone.sunk | while | flops 151388160 | bytes 2755167 | solution.py:23
  136.1 2.4 %fusion.154 = f32[6,128,128]{2,1,0:T(8,128)} fusion(f32[6,128,128]{2,1,0:T(8,128)S(1)} %copy.105, f32[4,6,128,128]{3,2,1,0:T(8,128)} %get-tuple-element.491, s32[]{:T(128)} %get-tuple-element.480, f32[4,6,128,128]{3,2,1,0:T(8,128)} %get-tuple-element.490, pred[]{:T(512)S(6)} %compare.4, pred[]{:T(512)S(6)} %lt.30), kind=kOutput, calls=%fused_computation.44.clone.1 | convolution fusion | flops 151388160 | bytes 1968640 | tf_op jit(solution)/shard_map/while/body/eval_jaxpr/hij,hjk->hik/dot_general | solution.py:80
  139.5 2.4 %fusion.154 = f32[6,128,128]{2,1,0:T(8,128)} fusion(f32[6,128,128]{2,1,0:T(8,128)S(1)} %copy.105, f32[4,6,128,128]{3,2,1,0:T(8,128)} %get-tuple-element.491, s32[]{:T(128)} %get-tuple-element.480, f32[4,6,128,128]{3,2,1,0:T(8,128)} %get-tuple-element.490, pred[]{:T(512)S(6)} %compare.4, pred[]{:T(512)S(6)} %lt.30), kind=kOutput, calls=%fused_computation.44.clone.1 | convolution fusion | flops 151388160 | bytes 1968640 | tf_op jit(solution)/shard_map/while/body/eval_jaxpr/hij,hjk->hik/dot_general | solution.py:80
  142.9 2.4 %fusion.154 = f32[6,128,128]{2,1,0:T(8,128)} fusion(f32[6,128,128]{2,1,0:T(8,128)S(1)} %copy.105, f32[4,6,128,128]{3,2,1,0:T(8,128)} %get-tuple-element.491, s32[]{:T(128)} %get-tuple-element.480, f32[4,6,128,128]{3,2,1,0:T(8,128)} %get-tuple-element.490, pred[]{:T(512)S(6)} %compare.4, pred[]{:T(512)S(6)} %lt.30), kind=kOutput, calls=%fused_computation.44.clone.1 | convolution fusion | flops 151388160 | bytes 1968640 | tf_op jit(solution)/shard_map/while/body/eval_jaxpr/hij,hjk->hik/dot_general | solution.py:80
  146.1 13.8 %while.39 = (s32[]{:T(128)}, f32[6,128,128]{2,1,0:T(8,128)}, f32[2,6,64,128]{3,2,1,0:T(8,128)}, f32[2,6,64,128]{3,2,1,0:T(8,128)}, f32[2,6,64,128]{3,2,1,0:T(8,1...) while((s32[]{:T(128)}, f32[6,128,128]{2,1,0:T(8,128)}, ...), condition=%wide.region_7.8_spmd, body=%wide.region_6.7_spmd.sunk | while | flops 264388608 | bytes 9046217 | solution.py:135
  146.1 1.6 fusion.149
  147.8 1.6 fusion.150
  150.5 2.6 %convolution_subtract_fusion.3 = f32[6,128,128]{2,1,0:T(8,128)} fusion(f32[6,128,128]{2,1,0:T(8,128)} %get-tuple-element.503, f32[6,64,128]{2,1,0:T(8,128)S(1)} %fusion.149, f32[2,6,64,128]{3,2,1,0:T(8,128)S(1)} %copy-done.4, s32[]{:T(128)} %get-tuple-element.502), kind=kOutput, calls=%fused_computation.25.clone.1 | convolution fusion | flops 75595776 | bytes 1179652 | tf_op jit(solution)/shard_map/while/body/eval_jaxpr/mjr,mjz->mrz/dot_general | solution.py:130
  153.0 1.6 fusion.149
  154.7 1.6 fusion.150
  157.4 2.6 %convolution_subtract_fusion.3 = f32[6,128,128]{2,1,0:T(8,128)} fusion(f32[6,128,128]{2,1,0:T(8,128)} %get-tuple-element.503, f32[6,64,128]{2,1,0:T(8,128)S(1)} %fusion.149, f32[2,6,64,128]{3,2,1,0:T(8,128)S(1)} %copy-done.4, s32[]{:T(128)} %get-tuple-element.502), kind=kOutput, calls=%fused_computation.25.clone.1 | convolution fusion | flops 75595776 | bytes 1179652 | tf_op jit(solution)/shard_map/while/body/eval_jaxpr/mjr,mjz->mrz/dot_general | solution.py:130
  160.0 1.9 %multiply_reduce_fusion = (f32[2,64,6]{1,2,0:T(8,128)S(1)}, f32[2,64,6,128]{3,1,2,0:T(8,128)}) fusion(f32[2,6,64,128]{3,2,1,0:T(8,128)} %get-tuple-element.179, f32[2,6,64,128]{3,2,1,0:T(8,128)} %get-tuple-element.182), kind=kLoop, calls=%fused_computation.77 | loop fusion | flops 294144 | bytes 1182720 | tf_op jit(solution)/shard_map/reduce_sum | solution.py:70
  162.8 1.9 %copy.63 = f32[128,768]{1,0:T(8,128)} copy(f32[128,768]{0,1:T(8,128)} %bitcast.156) | data formatting | bytes 786432 | tf_op jit(solution)/shard_map/mul | solution.py:71
  165.9 1.8 %fusion.56 = bf16[128,768]{1,0:T(8,128)(2,1)} fusion(f32[128,768]{1,0:T(8,128)} %copy.63, f32[16,8,6,128]{3,2,1,0:T(8,128)S(1)} %bitcast.154, f32[768]{0:T(1024)S(1)} %copy-done.12), kind=kLoop, calls=%fused_computation.73 | loop fusion | flops 294912 | bytes 986112 | tf_op jit(solution)/shard_map/convert_element_type | solution.py:72
  (93 shorter events, 37.9 us)
Async XLA Ops:
  6.5 12.3 %copy-start = (bf16[768,2304]{1,0:T(8,128)(2,1)S(1)}, bf16[768,2304]{1,0:T(8,128)(2,1)}, u32[]{:S(2)}) copy-start(bf16[768,2304]{1,0:T(8,128)(2,1)} %param.12) | copy-start | bytes 10616836
  8.3 10.5 %all-to-all-start = ((bf16[192,4,128]{2,0,1:T(8,128)(2,1)}), bf16[192,4,128]{2,0,1:T(8,128)(2,1)}, u32[]{:S(2)}, u32[]{:S(2)}) async-start(bf16[192,4,128]{2,0,1:T(8,128)(2,1)} %copy_bitcast_fusion), calls=%async_computation | async-start | bytes 393216 | tf_op jit(solution)/shard_map/all_to_all | solution.py:87
  13.5 88.9 %all-gather.5.cloned.1.call-start = ((), (), s32[]{:S(2)}) async-start(), calls=%async_computation.1 | async-start | bytes 1966080 | tf_op jit(solution)/shard_map/all_gather | solution.py:14
  35.2 2.1 %copy-start.11 = (pred[64,64]{1,0:T(8,128)(4,1)S(1)}, pred[64,64]{1,0:T(8,128)(4,1)}, u32[]{:S(2)}) copy-start(pred[64,64]{1,0:T(8,128)(4,1)} %iota_compare_fusion.2) | copy-start | bytes 12292
  37.3 1.9 %copy-start.1 = (f32[2,6,64,128]{3,2,1,0:T(8,128)}, f32[2,6,64,128]{3,2,1,0:T(8,128)S(1)}, u32[]{:S(2)}) copy-start(f32[2,6,64,128]{3,2,1,0:T(8,128)S(1)} %get-tuple-element.497) | copy-start | bytes 1179652
  37.3 1.9 %copy-start.10 = (f32[64,64]{1,0:T(8,128)S(1)}, f32[64,64]{1,0:T(8,128)}, u32[]{:S(2)}) copy-start(f32[64,64]{1,0:T(8,128)} %fusion.61) | copy-start | bytes 49156
  48.0 2.0 %copy-start.2 = (f32[2,6,64,128]{3,2,1,0:T(8,128)S(1)}, f32[2,6,64,128]{3,2,1,0:T(8,128)}, u32[]{:S(2)}) copy-start(f32[2,6,64,128]{3,2,1,0:T(8,128)} %copy-done.1) | copy-start | bytes 1179652
  52.3 2.9 %copy-start.5 = (f32[2,6,64,128]{3,2,1,0:T(8,128)S(1)}, f32[2,6,64,128]{3,2,1,0:T(8,128)}, u32[]{:S(2)}) copy-start(f32[2,6,64,128]{3,2,1,0:T(8,128)} %get-tuple-element.470) | copy-start | bytes 1179652 | tf_op jit(solution)/shard_map/while
  52.3 4.4 %copy-start.3 = (f32[2,6,64,128]{3,2,1,0:T(8,128)S(1)}, f32[2,6,64,128]{3,2,1,0:T(8,128)}, u32[]{:S(2)}) copy-start(f32[2,6,64,128]{3,2,1,0:T(8,128)} %get-tuple-element.467) | copy-start | bytes 1179652 | tf_op jit(solution)/shard_map/while
  55.1 4.4 %copy-start.6 = (f32[2,6,64,64]{3,2,1,0:T(8,128)S(1)}, f32[2,6,64,64]{3,2,1,0:T(8,128)}, u32[]{:S(2)}) copy-start(f32[2,6,64,64]{3,2,1,0:T(8,128)} %get-tuple-element.471) | copy-start | bytes 589828 | tf_op jit(solution)/shard_map/while
  60.6 2.9 %copy-start.5 = (f32[2,6,64,128]{3,2,1,0:T(8,128)S(1)}, f32[2,6,64,128]{3,2,1,0:T(8,128)}, u32[]{:S(2)}) copy-start(f32[2,6,64,128]{3,2,1,0:T(8,128)} %get-tuple-element.470) | copy-start | bytes 1179652 | tf_op jit(solution)/shard_map/while
  60.6 4.4 %copy-start.3 = (f32[2,6,64,128]{3,2,1,0:T(8,128)S(1)}, f32[2,6,64,128]{3,2,1,0:T(8,128)}, u32[]{:S(2)}) copy-start(f32[2,6,64,128]{3,2,1,0:T(8,128)} %get-tuple-element.467) | copy-start | bytes 1179652 | tf_op jit(solution)/shard_map/while
  63.4 4.4 %copy-start.6 = (f32[2,6,64,64]{3,2,1,0:T(8,128)S(1)}, f32[2,6,64,64]{3,2,1,0:T(8,128)}, u32[]{:S(2)}) copy-start(f32[2,6,64,64]{3,2,1,0:T(8,128)} %get-tuple-element.471) | copy-start | bytes 589828 | tf_op jit(solution)/shard_map/while
  71.0 64.1 %all-gather.7.cloned.1.call-start = ((), (), s32[]{:S(2)}) async-start(), calls=%async_computation.2 | async-start | bytes 1966080 | tf_op jit(solution)/shard_map/all_gather | solution.py:14
  146.1 3.2 %copy-start.7 = (f32[2,6,64,64]{3,2,1,0:T(8,128)S(1)}, f32[2,6,64,64]{3,2,1,0:T(8,128)}, u32[]{:S(2)}) copy-start(f32[2,6,64,64]{3,2,1,0:T(8,128)} %get-tuple-element.516) | copy-start | bytes 589828 | tf_op jit(solution)/shard_map/while
  146.1 3.3 %copy-start.8 = (f32[2,6,64,128]{3,2,1,0:T(8,128)S(1)}, f32[2,6,64,128]{3,2,1,0:T(8,128)}, u32[]{:S(2)}) copy-start(f32[2,6,64,128]{3,2,1,0:T(8,128)} %get-tuple-element.504) | copy-start | bytes 1179652 | tf_op jit(solution)/shard_map/while
  146.1 4.3 %copy-start.4 = (f32[2,6,64,128]{3,2,1,0:T(8,128)S(1)}, f32[2,6,64,128]{3,2,1,0:T(8,128)}, u32[]{:S(2)}) copy-start(f32[2,6,64,128]{3,2,1,0:T(8,128)} %get-tuple-element.513) | copy-start | bytes 1179652 | tf_op jit(solution)/shard_map/while
  149.7 0.8 copy-start.9
  153.0 3.2 %copy-start.7 = (f32[2,6,64,64]{3,2,1,0:T(8,128)S(1)}, f32[2,6,64,64]{3,2,1,0:T(8,128)}, u32[]{:S(2)}) copy-start(f32[2,6,64,64]{3,2,1,0:T(8,128)} %get-tuple-element.516) | copy-start | bytes 589828 | tf_op jit(solution)/shard_map/while
  153.0 3.3 %copy-start.8 = (f32[2,6,64,128]{3,2,1,0:T(8,128)S(1)}, f32[2,6,64,128]{3,2,1,0:T(8,128)}, u32[]{:S(2)}) copy-start(f32[2,6,64,128]{3,2,1,0:T(8,128)} %get-tuple-element.504) | copy-start | bytes 1179652 | tf_op jit(solution)/shard_map/while
  153.0 4.3 %copy-start.4 = (f32[2,6,64,128]{3,2,1,0:T(8,128)S(1)}, f32[2,6,64,128]{3,2,1,0:T(8,128)}, u32[]{:S(2)}) copy-start(f32[2,6,64,128]{3,2,1,0:T(8,128)} %get-tuple-element.513) | copy-start | bytes 1179652 | tf_op jit(solution)/shard_map/while
  156.6 0.8 copy-start.9
  160.0 6.0 %copy-start.12 = (f32[768]{0:T(1024)S(1)}, f32[768]{0:T(1024)}, u32[]{:S(2)}) copy-start(f32[768]{0:T(1024)} %param.15) | copy-start | bytes 9220
Sparse Core Ops, SparseCore 0:
  71.1 31.2 all-gather.4
  104.3 30.8 all-gather.6
where the time goes:
time: 176 us; the launch traced here: 175 us
  waiting for transfers between devices  65.4 us (37%)
  matrix products  46.7 us (27%)
  local copies, waits for them, and re-layouts  30.2 us (17%)
  between operations  13.6 us (8%)
  other arithmetic  13 us (7%)
  starting transfers between devices  5.42 us (3%)
    all_gather x2, waiting for transfers between devices, entering(): pieces = jax.tree.map(lambda part: lax.all_gather(part, axis), value)  63.4 us
    dot_general x3, matrix products, compose(): jnp.einsum('hij,hjk->hik', second_move, first_offset, precision=HIGHEST_A...  7.21 us
    dot_general x2, matrix products, first_pass(): jnp.einsum('mjr,mjz->mrz', key_block, target_value, precision=HIGHEST_ACC...  5.78 us
    all_to_all x1, starting transfers between devices, body(): lax.all_to_all(feats, 'seq', split_axis=1, concat_axis=0, tiled=True)  5.19 us
    dot_general x2, matrix products, second_pass(): jnp.einsum('mjr,mjz->mrz', key_block, held_value, precision=HIGHEST_ACCUR...  5.12 us
    while x31, local copies, waits for them, and re-layouts  4.53 us
    dot_general x2, matrix products, first_pass(): jnp.einsum('rnf,rfw->rnw', weight_block, joint_matrix, precision=HIGHEST_...  3.72 us
  transfers between devices with their start and end apart: 3, of which 3 were waited for; matrix products, arithmetic and copies ran while one was open for 2% of the time, Pallas kernels for 0%

commit v1 on v0

--- a/solution.py
+++ b/solution.py
@@ -1,3 +1,4 @@
+import functools
 import jax
 import jax.numpy as jnp
 from jax import lax
@@ -7,6 +8,22 @@
 HD = 128
 GROUP = 64
 HIGHEST_ACCURACY = lax.Precision.HIGHEST
+
+
+def _state_records(piece_in, bus_axis):
+    b_next = jnp.concatenate(
+        lax.all_to_all(
+            jnp.stack(jnp.split(piece_in, lax.axis_size(bus_axis), axis=1), axis=0),
+            axis_name=bus_axis,
+            split_axis=0,
+            concat_axis=0,
+        ),
+        axis=0,
+    )
+    return b_next
+
+
+track_cubes_all = functools.partial(_state_records, bus_axis="seq")
 
 
 def entering(value, axis, join, neutral):
@@ -84,7 +101,7 @@
 
 
 def body(feats, qkv_weight, beta_weight, beta_bias, out_gain):
-    local = lax.all_to_all(feats, "seq", split_axis=1, concat_axis=0, tiled=True)
+    local = track_cubes_all(feats)
     qkv = lax.dot_general(
         local, qkv_weight, (((0,), (0,)), ((), ())), preferred_element_type=jnp.float32
     ).astype(jnp.bfloat16)

time: 176 us -> 173 us (0.983)
  local copies, waits for them, and re-layouts: 30.2 us -> 28.1 us
    all_to_all x1 -> x0, local copies, waits for them, and re-layouts: 1.79 us -> none  [body(): lax.all_to_all(feats, 'seq', split_axis=1, concat_axis=0, tiled=True)]
  transfers between devices with their start and end apart: 3 -> 3, of which waited for: 3 -> 3; matrix products, arithmetic and copies ran while one was open for 2% -> 3% of each run, Pallas kernels for 0% -> 0%
where the time goes in v1:
time: 173 us; the launch traced here: 172 us
  waiting for transfers between devices  65.4 us (38%)
  matrix products  46 us (27%)
  local copies, waits for them, and re-layouts  28.1 us (16%)
  between operations  13.6 us (8%)
  other arithmetic  13.3 us (8%)
  starting transfers between devices  5.42 us (3%)
    all_gather x2, waiting for transfers between devices, entering(): pieces = jax.tree.map(lambda part: lax.all_gather(part, axis), value)  64 us
    dot_general x3, matrix products, compose(): jnp.einsum('hij,hjk->hik', second_move, first_offset, precision=HIGHEST_A...  7.23 us
    dot_general x2, matrix products, first_pass(): jnp.einsum('mjr,mjz->mrz', key_block, target_value, precision=HIGHEST_ACC...  5.78 us
    all_to_all x1, starting transfers between devices, _state_records(): lax.all_to_all(jnp.stack(jnp.split(piece_in, lax.axis_size(bus_axis), axi...  5.19 us
    dot_general x2, matrix products, second_pass(): jnp.einsum('mjr,mjz->mrz', key_block, held_value, precision=HIGHEST_ACCUR...  5.13 us
    while x31, local copies, waits for them, and re-layouts  4.54 us
    dot_general x2, matrix products, first_pass(): jnp.einsum('rnf,rfw->rnw', weight_block, joint_matrix, precision=HIGHEST_...  3.72 us
  transfers between devices with their start and end apart: 3, of which 3 were waited for; matrix products, arithmetic and copies ran while one was open for 3% of the time, Pallas kernels for 0%

profile of v1, /device:TPU:0, one launch (start us, length us, event | category | flops | bytes accessed | tf_op | source)
XLA Modules:
  0.0 172.0 jit_solution(11951028394643286616)
XLA Ops:
  8.3 5.2 %all-to-all-start = ((bf16[4,192,128]{2,1,0:T(8,128)(2,1)}), bf16[4,192,128]{2,1,0:T(8,128)(2,1)}, u32[]{:S(2)}, u32[]{:S(2)}) async-start(bf16[4,192,128]{2,1,0:T(8,128)(2,1)} %pad_maximum_fusion), calls=%async_computation | async-start | bytes 393216 | tf_op jit(solution)/shard_map/all_to_all | solution.py:15
  18.8 2.6 %fusion.45 = f32[128,2304]{1,0:T(8,128)} fusion(bf16[768,128]{1,0:T(8,128)(2,1)} %bitcast.15, bf16[768,2304]{1,0:T(8,128)(2,1)S(1)} %copy-done), kind=kOutput, calls=%fused_computation.53 | convolution fusion | flops 453574656 | bytes 4915200 | tf_op jit(solution)/shard_map/dot_general | solution.py:105
  21.4 2.7 %copy.34 = f32[128,2304]{0,1:T(8,128)} copy(f32[128,2304]{1,0:T(8,128)} %fusion.45) | data formatting | bytes 2359296 | tf_op jit(solution)/shard_map/reshape | solution.py:59
  24.1 2.3 %multiply_reduce_fusion.1 = (f32[128,6]{0,1:T(8,128)S(1)}, f32[128,6]{0,1:T(8,128)S(1)}, f32[128,1,6,128]{0,3,2,1:T(8,128)}, f32[128,1,6,128]{0,3,2,1:T(8,128)}, f32[128,1,6,128]{0,3,2,1:T(8,128)}) fusion(f32[128,3,6,128]{0,3,2,1:T(8,128)} %bitcast.152), kind=kLoop, calls=%fused_computation.80 | loop fusion | flops 391680 | bytes 2365440 | tf_op jit(solution)/shard_map/reduce_sum | solution.py:63
  27.0 1.9 %copy.35 = f32[128,1,6,128]{3,0,2,1:T(8,128)} copy(f32[128,1,6,128]{0,3,2,1:T(8,128)} %get-tuple-element.296) | data formatting | bytes 786432 | tf_op jit(solution)/shard_map/slice | solution.py:61
  28.9 1.9 %copy.39 = f32[128,1,6,128]{3,0,2,1:T(8,128)} copy(f32[128,1,6,128]{0,3,2,1:T(8,128)} %get-tuple-element.295) | data formatting | bytes 786432 | tf_op jit(solution)/shard_map/slice | solution.py:62
  34.7 1.9 %copy.41 = f32[128,1,6,128]{3,0,2,1:T(8,128)} copy(f32[128,1,6,128]{0,3,2,1:T(8,128)} %get-tuple-element.294) | data formatting | bytes 786432 | tf_op jit(solution)/shard_map/slice | solution.py:60
  38.9 1.5 convolution_select_fusion
  49.1 16.6 %while.38 = (s32[]{:T(128)}, f32[6,128,256]{2,1,0:T(8,128)}, f32[2,6,64,128]{3,2,1,0:T(8,128)}, f32[2,6,64,128]{3,2,1,0:T(8,128)}, f32[2,6,64,128]{3,2,1,0:T(8,1...) while((s32[]{:T(128)}, f32[6,128,256]{2,1,0:T(8,128)}, ...), condition=%wide.region_3.4_spmd, body=%wide.region_2.3_spmd.sunk | while | flops 415678464 | bytes 10029241 | solution.py:133
  49.1 1.9 %fusion.137 = f32[6,64,256]{2,1,0:T(8,128)S(1)} fusion(f32[6,128,256]{2,1,0:T(8,128)} %get-tuple-element.445, f32[2,6,64,128]{3,2,1,0:T(8,128)} %get-tuple-element.457, s32[]{:T(128)} %get-tuple-element.444), kind=kOutput, calls=%fused_computation.13.clone.1 | convolution fusion | flops 150994944 | bytes 1376768 | tf_op jit(solution)/shard_map/while/body/eval_jaxpr/rnf,rfw->rnw/dot_general | solution.py:118
  52.0 1.5 fusion.138
  53.5 2.9 %convolution_add_fusion.10 = f32[6,128,256]{2,1,0:T(8,128)} fusion(f32[6,128,256]{2,1,0:T(8,128)} %get-tuple-element.445, f32[6,64,128]{2,1,0:T(8,128)S(1)} %get-tuple-element.421, f32[6,64,128]{2,1,0:T(8,128)S(1)} %get-tuple-element.422, f32[2,6,64,128]{3,2,1,0:T(8,128)S(1)} %copy-done.2, s32[]{:T(128)} %get-tuple-element.444), kind=kOutput, calls=%fused_computation.clone.1 | convolution fusion | flops 151289856 | bytes 2162692 | tf_op jit(solution)/shard_map/while/body/eval_jaxpr/mjr,mjz->mrz/dot_general | solution.py:127
  57.4 1.9 %fusion.137 = f32[6,64,256]{2,1,0:T(8,128)S(1)} fusion(f32[6,128,256]{2,1,0:T(8,128)} %get-tuple-element.445, f32[2,6,64,128]{3,2,1,0:T(8,128)} %get-tuple-element.457, s32[]{:T(128)} %get-tuple-element.444), kind=kOutput, calls=%fused_computation.13.clone.1 | convolution fusion | flops 150994944 | bytes 1376768 | tf_op jit(solution)/shard_map/while/body/eval_jaxpr/rnf,rfw->rnw/dot_general | solution.py:118
  60.3 1.5 fusion.138
  61.8 2.9 %convolution_add_fusion.10 = f32[6,128,256]{2,1,0:T(8,128)} fusion(f32[6,128,256]{2,1,0:T(8,128)} %get-tuple-element.445, f32[6,64,128]{2,1,0:T(8,128)S(1)} %get-tuple-element.421, f32[6,64,128]{2,1,0:T(8,128)S(1)} %get-tuple-element.422, f32[2,6,64,128]{3,2,1,0:T(8,128)S(1)} %copy-done.2, s32[]{:T(128)} %get-tuple-element.444), kind=kOutput, calls=%fused_computation.clone.1 | convolution fusion | flops 151289856 | bytes 2162692 | tf_op jit(solution)/shard_map/while/body/eval_jaxpr/mjr,mjz->mrz/dot_general | solution.py:127
  65.7 2.1 %fusion.65 = (f32[6,128,128]{2,1,0:T(8,128)}, f32[6,128,128]{2,1,0:T(8,128)}) fusion(f32[6,128,256]{2,1,0:T(8,128)} %get-tuple-element.180), kind=kLoop, calls=%fused_computation.102 | loop fusion | bytes 1572864 | tf_op jit(solution)/shard_map/slice | solution.py:135
  68.6 31.2 %all-gather.5.cloned.1.call-done = f32[24,128,128]{2,1,0:T(8,128)} async-done(((f32[6,128,128]{2,1,0:T(8,128)}), f32[24,128,128]{2,1,0:T(8,128)}) %all-gather.5.cloned.1.call-update) | async-done | bytes 1572880 | tf_op jit(solution)/shard_map/all_gather | solution.py:31
  99.8 32.7 %all-gather.7.cloned.1.call-done = f32[24,128,128]{2,1,0:T(8,128)} async-done(((f32[6,128,128]{2,1,0:T(8,128)}), f32[24,128,128]{2,1,0:T(8,128)}) %all-gather.7.cloned.1.call-update) | async-done | bytes 1572880 | tf_op jit(solution)/shard_map/all_gather | solution.py:31
  132.5 10.2 %while.40 = (s32[]{:T(128)}, f32[6,128,128]{2,1,0:T(8,128)}, s32[]{:T(128)}, f32[4,6,128,128]{3,2,1,0:T(8,128)}, f32[4,6,128,128]{3,2,1,0:T(8,128)}, /*index=5*/s32[]{:T(128)}, s32[]{:T(128)}) while((s32[]{:T(128)}, f32[6,128,128]{2,1,0:T(8,128)}, s32[]{:T(128)}, f32[4,6,128,128]{3,2,1,0:T(8,128)}, f32[4,6,128,128]{3,2,1,0:T(8,128)}, ...), condition=%wide.region_5.6_spmd.clone, body=%wide.region_4.5_spmd.clone.sunk | while | flops 151388160 | bytes 2755167 | solution.py:40
  133.5 2.4 %fusion.153 = f32[6,128,128]{2,1,0:T(8,128)} fusion(f32[6,128,128]{2,1,0:T(8,128)S(1)} %copy.87, f32[4,6,128,128]{3,2,1,0:T(8,128)} %get-tuple-element.480, s32[]{:T(128)} %get-tuple-element.469, f32[4,6,128,128]{3,2,1,0:T(8,128)} %get-tuple-element.479, pred[]{:T(512)S(6)} %compare.4, pred[]{:T(512)S(6)} %lt.30), kind=kOutput, calls=%fused_computation.44.clone.1 | convolution fusion | flops 151388160 | bytes 1968640 | tf_op jit(solution)/shard_map/while/body/eval_jaxpr/hij,hjk->hik/dot_general | solution.py:97
  136.9 2.4 %fusion.153 = f32[6,128,128]{2,1,0:T(8,128)} fusion(f32[6,128,128]{2,1,0:T(8,128)S(1)} %copy.87, f32[4,6,128,128]{3,2,1,0:T(8,128)} %get-tuple-element.480, s32[]{:T(128)} %get-tuple-element.469, f32[4,6,128,128]{3,2,1,0:T(8,128)} %get-tuple-element.479, pred[]{:T(512)S(6)} %compare.4, pred[]{:T(512)S(6)} %lt.30), kind=kOutput, calls=%fused_computation.44.clone.1 | convolution fusion | flops 151388160 | bytes 1968640 | tf_op jit(solution)/shard_map/while/body/eval_jaxpr/hij,hjk->hik/dot_general | solution.py:97
  140.3 2.4 %fusion.153 = f32[6,128,128]{2,1,0:T(8,128)} fusion(f32[6,128,128]{2,1,0:T(8,128)S(1)} %copy.87, f32[4,6,128,128]{3,2,1,0:T(8,128)} %get-tuple-element.480, s32[]{:T(128)} %get-tuple-element.469, f32[4,6,128,128]{3,2,1,0:T(8,128)} %get-tuple-element.479, pred[]{:T(512)S(6)} %compare.4, pred[]{:T(512)S(6)} %lt.30), kind=kOutput, calls=%fused_computation.44.clone.1 | convolution fusion | flops 151388160 | bytes 1968640 | tf_op jit(solution)/shard_map/while/body/eval_jaxpr/hij,hjk->hik/dot_general | solution.py:97
  143.5 13.9 %while.39 = (s32[]{:T(128)}, f32[6,128,128]{2,1,0:T(8,128)}, f32[2,6,64,128]{3,2,1,0:T(8,128)}, f32[2,6,64,128]{3,2,1,0:T(8,128)}, f32[2,6,64,128]{3,2,1,0:T(8,1...) while((s32[]{:T(128)}, f32[6,128,128]{2,1,0:T(8,128)}, ...), condition=%wide.region_7.8_spmd, body=%wide.region_6.7_spmd.sunk | while | flops 264388608 | bytes 9046217 | solution.py:152
  143.6 1.6 fusion.148
  145.2 1.6 fusion.149
  147.9 2.6 %convolution_subtract_fusion.3 = f32[6,128,128]{2,1,0:T(8,128)} fusion(f32[6,128,128]{2,1,0:T(8,128)} %get-tuple-element.492, f32[6,64,128]{2,1,0:T(8,128)S(1)} %fusion.148, f32[2,6,64,128]{3,2,1,0:T(8,128)S(1)} %copy-done.3, s32[]{:T(128)} %get-tuple-element.491), kind=kOutput, calls=%fused_computation.25.clone.1 | convolution fusion | flops 75595776 | bytes 1179652 | tf_op jit(solution)/shard_map/while/body/eval_jaxpr/mjr,mjz->mrz/dot_general | solution.py:147
  150.5 1.6 fusion.148
  152.1 1.6 fusion.149
  154.8 2.6 %convolution_subtract_fusion.3 = f32[6,128,128]{2,1,0:T(8,128)} fusion(f32[6,128,128]{2,1,0:T(8,128)} %get-tuple-element.492, f32[6,64,128]{2,1,0:T(8,128)S(1)} %fusion.148, f32[2,6,64,128]{3,2,1,0:T(8,128)S(1)} %copy-done.3, s32[]{:T(128)} %get-tuple-element.491), kind=kOutput, calls=%fused_computation.25.clone.1 | convolution fusion | flops 75595776 | bytes 1179652 | tf_op jit(solution)/shard_map/while/body/eval_jaxpr/mjr,mjz->mrz/dot_general | solution.py:147
  157.4 2.0 %multiply_reduce_fusion = (f32[2,64,6]{1,2,0:T(8,128)S(1)}, f32[2,64,6,128]{3,1,2,0:T(8,128)}) fusion(f32[2,6,64,128]{3,2,1,0:T(8,128)} %get-tuple-element.179, f32[2,6,64,128]{3,2,1,0:T(8,128)} %get-tuple-element.182), kind=kLoop, calls=%fused_computation.77 | loop fusion | flops 294144 | bytes 1182720 | tf_op jit(solution)/shard_map/reduce_sum | solution.py:87
  160.2 1.9 %copy.47 = f32[128,768]{1,0:T(8,128)} copy(f32[128,768]{0,1:T(8,128)} %bitcast.157) | data formatting | bytes 786432 | tf_op jit(solution)/shard_map/mul | solution.py:88
  163.4 1.8 %fusion.56 = bf16[128,768]{1,0:T(8,128)(2,1)} fusion(f32[128,768]{1,0:T(8,128)} %copy.47, f32[16,8,6,128]{3,2,1,0:T(8,128)S(1)} %bitcast.155, f32[768]{0:T(1024)S(1)} %copy-done.14), kind=kLoop, calls=%fused_computation.73 | loop fusion | flops 294912 | bytes 986112 | tf_op jit(solution)/shard_map/convert_element_type | solution.py:89
  (98 shorter events, 35.2 us)
Async XLA Ops:
  6.5 12.2 %copy-start = (bf16[768,2304]{1,0:T(8,128)(2,1)S(1)}, bf16[768,2304]{1,0:T(8,128)(2,1)}, u32[]{:S(2)}) copy-start(bf16[768,2304]{1,0:T(8,128)(2,1)} %param.12) | copy-start | bytes 10616836
  8.3 10.5 %all-to-all-start = ((bf16[4,192,128]{2,1,0:T(8,128)(2,1)}), bf16[4,192,128]{2,1,0:T(8,128)(2,1)}, u32[]{:S(2)}, u32[]{:S(2)}) async-start(bf16[4,192,128]{2,1,0:T(8,128)(2,1)} %pad_maximum_fusion), calls=%async_computation | async-start | bytes 393216 | tf_op jit(solution)/shard_map/all_to_all | solution.py:15
  13.5 86.3 %all-gather.5.cloned.1.call-start = ((), (), s32[]{:S(2)}) async-start(), calls=%async_computation.1 | async-start | bytes 1966080 | tf_op jit(solution)/shard_map/all_gather | solution.py:31
  36.6 2.0 %copy-start.9 = (f32[128,1,6,128]{3,0,2,1:T(8,128)S(1)}, f32[128,1,6,128]{3,0,2,1:T(8,128)}, u32[]{:S(2)}) copy-start(f32[128,1,6,128]{3,0,2,1:T(8,128)} %copy.35) | copy-start | bytes 1179652
  36.6 2.0 %copy-start.10 = (f32[128,1,6,128]{3,0,2,1:T(8,128)S(1)}, f32[128,1,6,128]{3,0,2,1:T(8,128)}, u32[]{:S(2)}) copy-start(f32[128,1,6,128]{3,0,2,1:T(8,128)} %copy.39) | copy-start | bytes 1179652
  37.8 1.1 copy-start.13
  38.6 1.8 %copy-start.12 = (pred[64,64]{1,0:T(8,128)(4,1)S(1)}, pred[64,64]{1,0:T(8,128)(4,1)}, u32[]{:S(2)}) copy-start(pred[64,64]{1,0:T(8,128)(4,1)} %iota_compare_fusion.2) | copy-start | bytes 12292
  38.9 2.9 %copy-start.1 = (f32[2,6,64,128]{3,2,1,0:T(8,128)}, f32[2,6,64,128]{3,2,1,0:T(8,128)S(1)}, u32[]{:S(2)}) copy-start(f32[2,6,64,128]{3,2,1,0:T(8,128)S(1)} %get-tuple-element.486) | copy-start | bytes 1179652
  40.4 1.9 %copy-start.11 = (f32[64,64]{1,0:T(8,128)S(1)}, f32[64,64]{1,0:T(8,128)}, u32[]{:S(2)}) copy-start(f32[64,64]{1,0:T(8,128)} %fusion.61) | copy-start | bytes 49156
  49.1 2.9 %copy-start.4 = (f32[2,6,64,128]{3,2,1,0:T(8,128)S(1)}, f32[2,6,64,128]{3,2,1,0:T(8,128)}, u32[]{:S(2)}) copy-start(f32[2,6,64,128]{3,2,1,0:T(8,128)} %get-tuple-element.459) | copy-start | bytes 1179652 | tf_op jit(solution)/shard_map/while
  49.1 4.4 %copy-start.2 = (f32[2,6,64,128]{3,2,1,0:T(8,128)S(1)}, f32[2,6,64,128]{3,2,1,0:T(8,128)}, u32[]{:S(2)}) copy-start(f32[2,6,64,128]{3,2,1,0:T(8,128)} %get-tuple-element.456) | copy-start | bytes 1179652 | tf_op jit(solution)/shard_map/while
  52.0 4.4 %copy-start.5 = (f32[2,6,64,64]{3,2,1,0:T(8,128)S(1)}, f32[2,6,64,64]{3,2,1,0:T(8,128)}, u32[]{:S(2)}) copy-start(f32[2,6,64,64]{3,2,1,0:T(8,128)} %get-tuple-element.460) | copy-start | bytes 589828 | tf_op jit(solution)/shard_map/while
  57.4 2.9 %copy-start.4 = (f32[2,6,64,128]{3,2,1,0:T(8,128)S(1)}, f32[2,6,64,128]{3,2,1,0:T(8,128)}, u32[]{:S(2)}) copy-start(f32[2,6,64,128]{3,2,1,0:T(8,128)} %get-tuple-element.459) | copy-start | bytes 1179652 | tf_op jit(solution)/shard_map/while
  57.4 4.4 %copy-start.2 = (f32[2,6,64,128]{3,2,1,0:T(8,128)S(1)}, f32[2,6,64,128]{3,2,1,0:T(8,128)}, u32[]{:S(2)}) copy-start(f32[2,6,64,128]{3,2,1,0:T(8,128)} %get-tuple-element.456) | copy-start | bytes 1179652 | tf_op jit(solution)/shard_map/while
  60.3 4.4 %copy-start.5 = (f32[2,6,64,64]{3,2,1,0:T(8,128)S(1)}, f32[2,6,64,64]{3,2,1,0:T(8,128)}, u32[]{:S(2)}) copy-start(f32[2,6,64,64]{3,2,1,0:T(8,128)} %get-tuple-element.460) | copy-start | bytes 589828 | tf_op jit(solution)/shard_map/while
  67.8 64.7 %all-gather.7.cloned.1.call-start = ((), (), s32[]{:S(2)}) async-start(), calls=%async_computation.2 | async-start | bytes 1966080 | tf_op jit(solution)/shard_map/all_gather | solution.py:31
  143.5 3.2 %copy-start.6 = (f32[2,6,64,64]{3,2,1,0:T(8,128)S(1)}, f32[2,6,64,64]{3,2,1,0:T(8,128)}, u32[]{:S(2)}) copy-start(f32[2,6,64,64]{3,2,1,0:T(8,128)} %get-tuple-element.505) | copy-start | bytes 589828 | tf_op jit(solution)/shard_map/while
  143.5 3.3 %copy-start.7 = (f32[2,6,64,128]{3,2,1,0:T(8,128)S(1)}, f32[2,6,64,128]{3,2,1,0:T(8,128)}, u32[]{:S(2)}) copy-start(f32[2,6,64,128]{3,2,1,0:T(8,128)} %get-tuple-element.493) | copy-start | bytes 1179652 | tf_op jit(solution)/shard_map/while
  143.6 4.4 %copy-start.3 = (f32[2,6,64,128]{3,2,1,0:T(8,128)S(1)}, f32[2,6,64,128]{3,2,1,0:T(8,128)}, u32[]{:S(2)}) copy-start(f32[2,6,64,128]{3,2,1,0:T(8,128)} %get-tuple-element.502) | copy-start | bytes 1179652 | tf_op jit(solution)/shard_map/while
  147.1 0.8 copy-start.8
  150.5 3.2 %copy-start.6 = (f32[2,6,64,64]{3,2,1,0:T(8,128)S(1)}, f32[2,6,64,64]{3,2,1,0:T(8,128)}, u32[]{:S(2)}) copy-start(f32[2,6,64,64]{3,2,1,0:T(8,128)} %get-tuple-element.505) | copy-start | bytes 589828 | tf_op jit(solution)/shard_map/while
  150.5 3.3 %copy-start.7 = (f32[2,6,64,128]{3,2,1,0:T(8,128)S(1)}, f32[2,6,64,128]{3,2,1,0:T(8,128)}, u32[]{:S(2)}) copy-start(f32[2,6,64,128]{3,2,1,0:T(8,128)} %get-tuple-element.493) | copy-start | bytes 1179652 | tf_op jit(solution)/shard_map/while
  150.5 4.4 %copy-start.3 = (f32[2,6,64,128]{3,2,1,0:T(8,128)S(1)}, f32[2,6,64,128]{3,2,1,0:T(8,128)}, u32[]{:S(2)}) copy-start(f32[2,6,64,128]{3,2,1,0:T(8,128)} %get-tuple-element.502) | copy-start | bytes 1179652 | tf_op jit(solution)/shard_map/while
  154.1 0.8 copy-start.8
  157.4 6.0 %copy-start.14 = (f32[768]{0:T(1024)S(1)}, f32[768]{0:T(1024)}, u32[]{:S(2)}) copy-start(f32[768]{0:T(1024)} %param.15) | copy-start | bytes 9220
Sparse Core Ops, SparseCore 0:
  67.9 31.8 all-gather.4
  101.7 30.8 all-gather.6
